TPU v7x, 32 devices: a whole 2x2x4 slice. The times are simulated.
32 devices in a mesh: groups: 2 (over y), video: 4 (over z), tensor: 4 (over x, core).
Axes of the slice: x: 2, y: 2, z: 4, core: 2. Of those that a mesh axis runs over, the one named last changes fastest.
Arguments:
- frames: bfloat16 [24, 256, 6144], P(('groups', 'video')), parts along dimension 0, may hold values from -610 to 610
- frame_video: int32 [24], P(('groups', 'video')), parts along dimension 0, may hold values from 0 to 3, never falling along the last dimension, each value on 1 to 6 neighbouring positions
- qkv_weight: bfloat16 [6144, 3, 3072], P('video', None, 'tensor'), may hold values from -0.078125 to 0.078125
- conn_weight: bfloat16 [3072, 3, 4096], P('tensor', None, 'video'), may hold values from -6 to 6
Outputs:
- summary: bfloat16 [384, 4096], P(('groups', 'video'), 'tensor'), parts along dimension 0
There are 2 independent parts, one for each index of `groups`. A program takes and returns all parts, laid end to end along the dimension named above; an argument that names none is the same for every part. Nothing has to cross between parts.
All inputs are finite; a program needn't handle non-finite values.
Results may differ from a plain program's by a relative error of at most 0.009.
Values may be sent and summed in bfloat16 or wider, within the bound.
No kernel may reach another device: no remote copies, remote signals or barrier semaphores. Data moves between devices by JAX's collectives and lax.ppermute only.
A program may use at most 192 MiB of HBM per device.

v0:
```python
import math
import jax
import jax.numpy as jnp
from jax import lax
from jax.sharding import PartitionSpec as P

HD = 128
PATCH = 256
POOL = 16


def rms_norm(values):
    return values * lax.rsqrt(jnp.mean(values * values, axis=-1, keepdims=True) + 1e-06)


def head_chunks(heads):
    if heads >= 4 and heads % 2 == 0:
        return [1] + [2] * ((heads - 2) // 2) + [1]
    return [1] * heads


def moved_weights(chunk, n_video, after=None):
    v = lax.axis_index("video")
    g = lax.axis_index("groups")
    half = chunk.shape[0] // 2
    mine = lax.dynamic_slice_in_dim(chunk, g * half, half, axis=0)
    if after is not None:
        mine, after = lax.optimization_barrier((mine, after))
    other = lax.dynamic_slice_in_dim(chunk, (1 - g) * half, half, axis=0)
    gathered = lax.all_gather(mine, "video", axis=0, tiled=True)
    onward = jnp.concatenate(
        [
            lax.dynamic_slice_in_dim(gathered, (v + 1 + i) % n_video * half, half, axis=0)
            for i in range(n_video - 1)
        ],
        axis=0,
    )
    return ([other, gathered, onward], after)


def forward(onward):
    return lax.ppermute(onward, "groups", [(0, 1), (1, 0)])


def attend(proj, nframes, heads, scale, blocks, inner):
    proj = proj.reshape(nframes, PATCH, 3, heads, HD)
    query = rms_norm(proj[:, :, 0]).astype(jnp.bfloat16)
    keys = rms_norm(proj[:, :, 1]).astype(jnp.bfloat16)
    values = proj[:, :, 2].astype(jnp.bfloat16)
    scores = jnp.einsum("fphd,fkhd->fhpk", query, keys, preferred_element_type=jnp.float32) * scale
    probs = jnp.exp(scores)
    probs = (probs / jnp.sum(probs, axis=-1, keepdims=True)).astype(jnp.bfloat16)
    attended = jnp.einsum("fhpk,fkhd->fphd", probs, values, preferred_element_type=jnp.float32)
    grid = attended.reshape(nframes, blocks, inner, blocks, inner, heads, HD)
    return jnp.mean(grid, axis=(2, 4)).reshape(nframes * POOL, heads * HD).astype(jnp.bfloat16)


def per_device(frames, frame_video, qkv_weight, conn_weight):
    scale = 1.0 / math.sqrt(HD)
    blocks = math.isqrt(POOL)
    inner = math.isqrt(PATCH) // blocks
    nframes = frames.shape[0]
    patch_rows = nframes * PATCH
    n_video = lax.axis_size("video")
    assert lax.axis_size("groups") == 2
    v = lax.axis_index("video")
    g = lax.axis_index("groups")
    heads_local = qkv_weight.shape[2] // HD
    sizes = head_chunks(heads_local)
    moved = []
    first = 0
    for size in sizes:
        chunk = qkv_weight[:, :, first * HD : (first + size) * HD]
        first += size
        if len(moved) == len(sizes) - 1 and len(sizes) > 2:
            whole_rows, moved[-1][1] = lax.optimization_barrier((chunk, moved[-1][1]))
            step = [lax.all_gather(whole_rows, "video", axis=0, tiled=True), None, None]
        elif moved:
            step, moved[-1][1] = moved_weights(chunk, n_video, after=moved[-1][1])
            step.append(forward(step[2]))
        else:
            step, _ = moved_weights(chunk, n_video)
            step.append(forward(step[2]))
            step[3], frames = lax.optimization_barrier((step[3], frames))
        moved.append(step)
    wide = frames.astype(jnp.float32)
    center = wide - jnp.mean(wide, axis=-1, keepdims=True)
    normed = center * lax.rsqrt(jnp.mean(center * center, axis=-1, keepdims=True) + 1e-06)
    normed = normed.astype(jnp.bfloat16).reshape(patch_rows, frames.shape[2])
    local_rows = qkv_weight.shape[0]
    half = local_rows // 2

    def columns(shard, which):
        return lax.dynamic_slice_in_dim(normed, shard * local_rows + which * half, half, axis=1)

    own_half = jnp.concatenate([columns(u, g) for u in range(n_video)], axis=1)
    own_piece = columns(v, 1 - g)
    rolled = jnp.concatenate(
        [columns((v + 1 + i) % n_video, 1 - g) for i in range(n_video - 1)], axis=1
    )
    if len(moved) > 2 and moved[1][3] is not None:
        moved[1][3], own_half = lax.optimization_barrier((moved[1][3], own_half))
    ids = [frame_video] + [
        lax.ppermute(frame_video, "video", [(a, (a + k) % n_video) for a in range(n_video)])
        for k in range(1, n_video)
    ]
    ids_from = jnp.argsort(jnp.stack([(v - k) % n_video for k in range(n_video)]))
    video_all = jnp.take(jnp.stack(ids), ids_from, axis=0).reshape(-1)
    pooled_parts = []
    for index, size in enumerate(sizes):
        width = 3 * size * HD
        if moved[index][1] is None:
            full = moved[index][0].reshape(n_video * 2 * half, width)
            proj = jnp.dot(normed, full, preferred_element_type=jnp.float32)
            pooled_parts.append(attend(proj, nframes, size, scale, blocks, inner))
            continue
        other, gathered, onward, received = moved[index]
        if index == 0:
            video_all, received = lax.optimization_barrier((video_all, received))
        proj = jnp.dot(own_piece, other.reshape(half, width), preferred_element_type=jnp.float32)
        proj = proj + jnp.dot(
            own_half, gathered.reshape(n_video * half, width), preferred_element_type=jnp.float32
        )
        proj = proj + jnp.dot(
            rolled,
            received.reshape((n_video - 1) * half, width),
            preferred_element_type=jnp.float32,
        )
        pooled_parts.append(attend(proj, nframes, size, scale, blocks, inner))
    pooled = jnp.concatenate(pooled_parts, axis=1)
    shifted = [pooled] + [
        lax.ppermute(pooled, "video", [(a, (a + k) % n_video) for a in range(n_video)])
        for k in range(1, n_video)
    ]
    came_from = jnp.argsort(jnp.stack([(v - k) % n_video for k in range(n_video)]))
    pooled_all = jnp.take(jnp.stack(shifted), came_from, axis=0).reshape(-1, pooled.shape[1])
    rows = pooled_all.shape[0]
    partial_proj = jnp.einsum(
        "rc,ckt->rkt", pooled_all, conn_weight, preferred_element_type=jnp.float32
    )
    n_tensor = lax.axis_size("tensor")
    t = lax.axis_index("tensor")
    sent = partial_proj.astype(jnp.bfloat16)
    block = rows // n_tensor
    total = lax.dynamic_slice_in_dim(sent, t * block, block, axis=0).astype(jnp.float32)
    for k in range(1, n_tensor):
        piece = lax.dynamic_slice_in_dim(sent, (t + k) % n_tensor * block, block, axis=0)
        got = lax.ppermute(piece, "tensor", [(a, (a + k) % n_tensor) for a in range(n_tensor)])
        total = total + got.astype(jnp.float32)
    clip_rows = total.astype(jnp.bfloat16)
    if n_video == n_tensor:
        pieces = [None] * n_tensor
        for k in range(n_tensor):
            pairs = [
                (a * n_tensor + b, (b + k) % n_tensor * n_tensor + a)
                for a in range(n_video)
                for b in range(n_tensor)
            ]
            got = lax.ppermute(clip_rows, ("video", "tensor"), pairs)
            pieces[k] = got
        source = [(v - k) % n_tensor for k in range(n_tensor)]
        stacked = jnp.stack(pieces, axis=0)
        order = jnp.argsort(jnp.stack(source))
        clip_proj = jnp.take(stacked, order, axis=0).reshape(rows, 3, -1).astype(jnp.float32)
    else:
        clip_rows = lax.all_gather(clip_rows, "video", axis=0, tiled=False)
        sub = n_video // n_tensor
        clip_rows = clip_rows.reshape((n_tensor, sub) + clip_rows.shape[1:])
        clip_proj = lax.all_to_all(clip_rows, "tensor", 0, 0, tiled=False)
        clip_proj = jnp.transpose(clip_proj, (0, 2, 3, 1, 4))
        clip_proj = clip_proj.reshape(rows, 3, -1).astype(jnp.float32)
    t_heads = clip_proj.shape[2] // HD
    out_rows = rows // n_video
    start = v * out_rows
    own = lax.dynamic_slice_in_dim(clip_proj[:, 0], start, out_rows, axis=0)
    tquery = rms_norm(own.reshape(out_rows, t_heads, HD)).astype(jnp.bfloat16)
    tkey = rms_norm(clip_proj[:, 1].reshape(rows, t_heads, HD)).astype(jnp.bfloat16)
    tvalue = clip_proj[:, 2].reshape(rows, t_heads, HD).astype(jnp.bfloat16)
    seg_rows = jnp.repeat(video_all, POOL)
    row_frame = jnp.arange(rows, dtype=jnp.int32) // POOL
    own_seg = lax.dynamic_slice_in_dim(seg_rows, start, out_rows)
    own_frame = lax.dynamic_slice_in_dim(row_frame, start, out_rows)
    allowed = (seg_rows[None, :] == own_seg[:, None]) & (row_frame[None, :] <= own_frame[:, None])
    logits = jnp.einsum("rhd,khd->hrk", tquery, tkey, preferred_element_type=jnp.float32) * scale
    weights = jnp.where(allowed[None], jnp.exp(logits), jnp.float32(0.0))
    numer = jnp.einsum(
        "hrk,khd->rhd", weights.astype(jnp.bfloat16), tvalue, preferred_element_type=jnp.float32
    )
    denom = jnp.sum(weights, axis=-1)
    summary = numer / jnp.transpose(denom)[:, :, None]
    return summary.reshape(out_rows, t_heads * HD).astype(jnp.bfloat16)


def solution(mesh):
    return jax.shard_map(
        per_device,
        mesh=mesh,
        in_specs=(
            P(("groups", "video"), None, None),
            P(("groups", "video")),
            P("video", None, "tensor"),
            P("tensor", None, "video"),
        ),
        out_specs=P(("groups", "video"), "tensor"),
        check_vma=False,
    )
```

profile of v0, /device:TPU:10, one launch (start us, length us, event | category | flops | bytes accessed | tf_op | source)
XLA Modules:
  0.0 423.8 jit_solution(11651524342442306222)
XLA Ops:
  18.0 43.6 %all-gather.5.cloned.1.call-done = bf16[3072,3,128]{0,2,1:T(8,128)(2,1)} async-done(((bf16[768,3,128]{0,2,1:T(8,128)(2,1)}), bf16[3072,3,128]{0,2,1:T(8,128)(2,1)}) %all-gather.5.cloned.1.call-update) | async-done | bytes 2359312 | tf_op jit(solution)/shard_map/all_gather | solution.py:30
  68.2 3.5 collective-permute-start.3
  82.2 22.9 %collective-permute-done = bf16[2304,3,128]{0,2,1:T(8,128)(2,1)} collective-permute-done((bf16[2304,3,128]{0,2,1:T(8,128)(2,1)}, bf16[2304,3,128]{0,2,1:T(8,128)(2,1)}, u32[]{:S(2)}, u32[]{:S(2)}) %collective-permute-start) | collective-permute-done | bytes 1769504 | tf_op jit(solution)/shard_map/ppermute | solution.py:42
  105.0 5.1 %convert_reduce_fusion = f32[3,256]{1,0:T(4,128)S(1)} fusion(bf16[3,256,6144]{2,1,0:T(8,128)(2,1)} %param.4), kind=kLoop, calls=%fused_computation.4 | loop fusion | flops 9436416 | bytes 9440256 | tf_op jit(solution)/shard_map/reduce_sum | solution.py:87
  110.2 6.3 %fusion.2 = f32[3,256]{1,0:T(4,128)S(1)} fusion(bf16[3,256,6144]{2,1,0:T(8,128)(2,1)} %param.4, f32[3,256]{1,0:T(4,128)S(1)} %broadcast_multiply_fusion), kind=kLoop, calls=%fused_computation.7 | loop fusion | flops 18873600 | bytes 9443328 | tf_op jit(solution)/shard_map/reduce_sum | solution.py:88
  116.5 34.0 %all-gather.7.cloned.1.call-done = bf16[3072,3,256]{0,2,1:T(8,128)(2,1)} async-done(((bf16[768,3,256]{0,2,1:T(8,128)(2,1)}), bf16[3072,3,256]{0,2,1:T(8,128)(2,1)}) %all-gather.7.cloned.1.call-update) | async-done | bytes 4718608 | tf_op jit(solution)/shard_map/all_gather | solution.py:30
  155.1 12.2 %fusion.3 = bf16[3,256,6144]{2,1,0:T(8,128)(2,1)} fusion(bf16[3,256,6144]{2,1,0:T(8,128)(2,1)} %param.4, f32[3,256]{1,0:T(4,128)S(1)} %add_rsqrt_fusion.10, f32[3,256]{1,0:T(4,128)S(1)} %broadcast_multiply_fusion), kind=kLoop, calls=%fused_computation.8 | loop fusion | flops 18874368 | bytes 18880512 | tf_op jit(solution)/shard_map/convert_element_type | solution.py:89
  169.7 4.0 fusion.22
  173.7 3.8 fusion.20
  183.3 3.7 fusion.65
  186.9 45.1 %collective-permute-done.1 = bf16[2304,3,256]{0,2,1:T(8,128)(2,1)} collective-permute-done((bf16[2304,3,256]{0,2,1:T(8,128)(2,1)S(1)}, bf16[2304,3,256]{0,2,1:T(8,128)(2,1)}, u32[]{:S(2)}, u32[]{:S(2)}) %collective-permute-start.1) | collective-permute-done | bytes 3538976 | tf_op jit(solution)/shard_map/ppermute | solution.py:42
  236.2 3.3 multiply_reduce_fusion.8
  240.4 7.1 %fusion.72 = f32[768,768]{1,0:T(8,128)S(1)} fusion(bf16[768,3072]{1,0:T(8,128)(2,1)} %copy-done.1, bf16[3072,768]{0,1:T(8,128)(2,1)} %bitcast.191), kind=kOutput, calls=%fused_computation.180 | convolution fusion | flops 3623878656 | bytes 11796480 | tf_op jit(solution)/shard_map/dot_general | solution.py:121
  253.9 6.6 %add_add_fusion.1 = f32[768,768]{1,0:T(8,128)} fusion(f32[768,768]{1,0:T(8,128)S(1)} %copy-done.19, f32[768,768]{1,0:T(8,128)S(1)} %fusion.72, bf16[2304,768]{0,1:T(8,128)(2,1)} %bitcast.21, bf16[768,768]{1,0:T(8,128)(2,1)S(1)} %copy-done.10, bf16[768,768]{1,0:T(8,128)(2,1)S(1)} %copy-done.13, bf16[768,768]{1,0:T(8,128)(2,1)S(1)} %copy-done.7), kind=kOutput, calls=%fused_computation.17 | convolution fusion | flops 2729705472 | bytes 14155776 | tf_op jit(solution)/shard_map/dot_general | solution.py:124
  267.5 7.5 %fusion.73 = f32[768,768]{1,0:T(8,128)S(1)} fusion(bf16[768,3072]{1,0:T(8,128)(2,1)} %copy-done.1, bf16[3072,768]{0,1:T(8,128)(2,1)} %bitcast.192), kind=kOutput, calls=%fused_computation.181 | convolution fusion | flops 3623878656 | bytes 11796480 | tf_op jit(solution)/shard_map/dot_general | solution.py:121
  275.0 54.6 %collective-permute-done.5 = bf16[2304,3,256]{0,2,1:T(8,128)(2,1)} collective-permute-done((bf16[2304,3,256]{0,2,1:T(8,128)(2,1)}, bf16[2304,3,256]{0,2,1:T(8,128)(2,1)}, u32[]{:S(2)}, u32[]{:S(2)}) %collective-permute-start.5) | collective-permute-done | bytes 3538976 | tf_op jit(solution)/shard_map/ppermute | solution.py:42
  329.6 6.4 %add_add_fusion = f32[768,768]{1,0:T(8,128)} fusion(f32[768,768]{1,0:T(8,128)S(1)} %copy-done.18, f32[768,768]{1,0:T(8,128)S(1)} %fusion.73, bf16[2304,768]{0,1:T(8,128)(2,1)} %bitcast.29, bf16[768,768]{1,0:T(8,128)(2,1)S(1)} %copy-done.11, bf16[768,768]{1,0:T(8,128)(2,1)S(1)} %copy-done.14, bf16[768,768]{1,0:T(8,128)(2,1)S(1)} %copy-done.8), kind=kOutput, calls=%fused_computation.16 | convolution fusion | flops 2729705472 | bytes 14155776 | tf_op jit(solution)/shard_map/dot_general | solution.py:124
  342.8 11.0 %fusion.7 = f32[3,256,3,1,128]{1,4,2,0,3:T(8,128)S(1)} fusion(bf16[6144,3,128]{0,2,1:T(8,128)(2,1)} %all-gather.11.cloned.1.call-done, bf16[3,256,6144]{2,1,0:T(8,128)(2,1)} %fusion.3), kind=kOutput, calls=%fused_computation.24 | convolution fusion | flops 3623878656 | bytes 15335424 | tf_op jit(solution)/shard_map/dot_general | solution.py:114
  365.5 3.5 convolution_convert_fusion
  370.3 8.8 %collective-permute-done.10 = bf16[48,3,1024]{2,0,1:T(8,128)(2,1)S(1)} collective-permute-done((bf16[48,3,1024]{2,0,1:T(8,128)(2,1)S(1)}, bf16[48,3,1024]{2,0,1:T(8,128)(2,1)S(1)}, u32[]{:S(2)}, u32[]{:S(2)}) %collective-permute-start.10) | collective-permute-done | bytes 294944 | tf_op jit(solution)/shard_map/ppermute | solution.py:148
  380.5 3.4 collective-permute-start.12
  384.0 3.4 collective-permute-start.13
  388.4 14.1 %collective-permute-done.12 = bf16[48,3,1024]{2,0,1:T(8,128)(2,1)S(1)} collective-permute-done((bf16[48,3,1024]{2,0,1:T(8,128)(2,1)S(1)}, bf16[48,3,1024]{2,0,1:T(8,128)(2,1)S(1)}, u32[]{:S(2)}, u32[]{:S(2)}) %collective-permute-start.12) | collective-permute-done | bytes 294944 | tf_op jit(solution)/shard_map/ppermute | solution.py:159
  402.5 9.1 %collective-permute-done.13 = bf16[48,3,1024]{2,0,1:T(8,128)(2,1)S(1)} collective-permute-done((bf16[48,3,1024]{2,0,1:T(8,128)(2,1)S(1)}, bf16[48,3,1024]{2,0,1:T(8,128)(2,1)S(1)}, u32[]{:S(2)}, u32[]{:S(2)}) %collective-permute-start.13) | collective-permute-done | bytes 294944 | tf_op jit(solution)/shard_map/ppermute | solution.py:159
  (192 shorter events, 86.7 us)
Async XLA Ops:
  6.5 55.0 %all-gather.5.cloned.1.call-start = ((), (), s32[]{:S(2)}) async-start(), calls=%async_computation | async-start | bytes 2949120 | tf_op jit(solution)/shard_map/all_gather | solution.py:30
  11.4 139.1 %all-gather.7.cloned.1.call-start = ((), (), s32[]{:S(2)}) async-start(), calls=%async_computation.1 | async-start | bytes 5898240 | tf_op jit(solution)/shard_map/all_gather | solution.py:30
  61.6 186.0 %all-gather.9.cloned.1.call-start = ((), (), s32[]{:S(2)}) async-start(), calls=%async_computation.2 | async-start | bytes 5898240 | tf_op jit(solution)/shard_map/all_gather | solution.py:30
  64.6 40.4 %collective-permute-start = (bf16[2304,3,128]{0,2,1:T(8,128)(2,1)}, bf16[2304,3,128]{0,2,1:T(8,128)(2,1)}, u32[]{:S(2)}, u32[]{:S(2)}) collective-permute-start(bf16[2304,3,128]{0,2,1:T(8,128)(2,1)} %pad_maximum_fusion.4), channel_id=1, source_target_pairs={{0,16},{16,0},{1,17},{17,1},{2,18},{18,2},{3,19},{19,3},{4,20},{20... | collective-permute-start | bytes 5308424 | tf_op jit(solution)/shard_map/ppermute | solution.py:42
  66.1 14.8 %collective-permute-start.4 = (s32[3]{0:T(128)S(1)}, s32[3]{0:T(128)S(1)}, u32[]{:S(2)}, u32[]{:S(2)}) collective-permute-start(s32[3]{0:T(128)S(1)} %copy-done.17), channel_id=1, source_target_pairs={{0,12},{4,0},{8,4},{12,8},{1,13},{5,1},{9,5},{13,9},{2,14},{6,2},{... | collective-permute-start | bytes 44 | tf_op jit(solution)/shard_map/ppermute | solution.py:104
  68.2 12.7 %collective-permute-start.2 = (s32[3]{0:T(128)S(1)}, s32[3]{0:T(128)S(1)}, u32[]{:S(2)}, u32[]{:S(2)}) collective-permute-start(s32[3]{0:T(128)S(1)} %copy-done.17), channel_id=1, source_target_pairs={{0,4},{4,8},{8,12},{12,0},{1,5},{5,9},{9,13},{13,1},{2,6},{6,10},{... | collective-permute-start | bytes 44 | tf_op jit(solution)/shard_map/ppermute | solution.py:104
  68.2 12.7 %collective-permute-start.3 = (s32[3]{0:T(128)S(1)}, s32[3]{0:T(128)}, u32[]{:S(2)}, u32[]{:S(2)}) collective-permute-start(s32[3]{0:T(128)S(1)} %copy-done.17), channel_id=1, source_target_pairs={{0,8},{4,12},{8,0},{12,4},{1,9},{5,13},{9,1},{13,5},{2,10},{6,14},... | collective-permute-start | bytes 44 | tf_op jit(solution)/shard_map/ppermute | solution.py:104
  150.5 192.3 %all-gather.11.cloned.1.call-start = ((), (), s32[]{:S(2)}) async-start(), calls=%async_computation.3 | async-start | bytes 5898240 | tf_op jit(solution)/shard_map/all_gather | solution.py:77
  153.6 78.4 %collective-permute-start.1 = (bf16[2304,3,256]{0,2,1:T(8,128)(2,1)S(1)}, bf16[2304,3,256]{0,2,1:T(8,128)(2,1)}, u32[]{:S(2)}, u32[]{:S(2)}) collective-permute-start(bf16[2304,3,256]{0,2,1:T(8,128)(2,1)S(1)} %pad_maximum_fusion.1), channel_id=1, source_target_pairs={{0,16},{16,0},{1,17},{17,1},{2,18},{18,2},{3,19},{19,3},{4,20},{20... | collective-permute-start | bytes 10616840 | tf_op jit(solution)/shard_map/ppermute | solution.py:42
  251.8 77.7 %collective-permute-start.5 = (bf16[2304,3,256]{0,2,1:T(8,128)(2,1)}, bf16[2304,3,256]{0,2,1:T(8,128)(2,1)}, u32[]{:S(2)}, u32[]{:S(2)}) collective-permute-start(bf16[2304,3,256]{0,2,1:T(8,128)(2,1)} %pad_maximum_fusion.3), channel_id=1, source_target_pairs={{0,16},{16,0},{1,17},{17,1},{2,18},{18,2},{3,19},{19,3},{4,20},{20... | collective-permute-start | bytes 10616840 | tf_op jit(solution)/shard_map/ppermute | solution.py:42
  267.4 62.1 %copy-start.8 = (bf16[768,768]{1,0:T(8,128)(2,1)S(1)}, bf16[768,768]{1,0:T(8,128)(2,1)}, u32[]{:S(2)}) copy-start(bf16[768,768]{1,0:T(8,128)(2,1)} %copy-done.6) | copy-start | bytes 3538948
  267.4 62.1 %copy-start.11 = (bf16[768,768]{1,0:T(8,128)(2,1)S(1)}, bf16[768,768]{1,0:T(8,128)(2,1)}, u32[]{:S(2)}) copy-start(bf16[768,768]{1,0:T(8,128)(2,1)} %get-tuple-element.38) | copy-start | bytes 3538948
  267.4 62.1 %copy-start.14 = (bf16[768,768]{1,0:T(8,128)(2,1)S(1)}, bf16[768,768]{1,0:T(8,128)(2,1)}, u32[]{:S(2)}) copy-start(bf16[768,768]{1,0:T(8,128)(2,1)} %get-tuple-element.39) | copy-start | bytes 3538948
  267.5 62.1 %copy-start.18 = (f32[768,768]{1,0:T(8,128)S(1)}, f32[768,768]{1,0:T(8,128)}, u32[]{:S(2)}) copy-start(f32[768,768]{1,0:T(8,128)} %fusion.20) | copy-start | bytes 7077892
  354.8 6.5 %collective-permute-start.6 = (bf16[48,768]{1,0:T(8,128)(2,1)S(1)}, bf16[48,768]{1,0:T(8,128)(2,1)S(1)}, u32[]{:S(2)}, u32[]{:S(2)}) collective-permute-start(bf16[48,768]{1,0:T(8,128)(2,1)S(1)} %get-tuple-element.73), channel_id=1, source_target_pairs={{0,4},{4,8},{8,12},{12,0},{1,5},{5,9},{9,13},{13,1},{2,6},{6,10},{... | collective-permute-start | bytes 221192 | tf_op jit(solution)/shard_map/ppermute | solution.py:132
  357.3 6.4 %collective-permute-start.7 = (bf16[48,768]{1,0:T(8,128)(2,1)S(1)}, bf16[48,768]{1,0:T(8,128)(2,1)S(1)}, u32[]{:S(2)}, u32[]{:S(2)}) collective-permute-start(bf16[48,768]{1,0:T(8,128)(2,1)S(1)} %get-tuple-element.73), channel_id=1, source_target_pairs={{0,8},{4,12},{8,0},{12,4},{1,9},{5,13},{9,1},{13,5},{2,10},{6,14},... | collective-permute-start | bytes 221192 | tf_op jit(solution)/shard_map/ppermute | solution.py:132
  360.5 4.4 %collective-permute-start.8 = (bf16[48,768]{1,0:T(8,128)(2,1)S(1)}, bf16[48,768]{1,0:T(8,128)(2,1)S(1)}, u32[]{:S(2)}, u32[]{:S(2)}) collective-permute-start(bf16[48,768]{1,0:T(8,128)(2,1)S(1)} %get-tuple-element.73), channel_id=1, source_target_pairs={{0,12},{4,0},{8,4},{12,8},{1,13},{5,1},{9,5},{13,9},{2,14},{6,2},{... | collective-permute-start | bytes 221192 | tf_op jit(solution)/shard_map/ppermute | solution.py:132
  369.1 9.9 %collective-permute-start.10 = (bf16[48,3,1024]{2,0,1:T(8,128)(2,1)S(1)}, bf16[48,3,1024]{2,0,1:T(8,128)(2,1)S(1)}, u32[]{:S(2)}, u32[]{:S(2)}) collective-permute-start(bf16[48,3,1024]{2,0,1:T(8,128)(2,1)S(1)} %get-tuple-element.69), channel_id=1, source_target_pairs={{0,2},{1,3},{2,0},{3,1},{4,6},{5,7},{6,4},{7,5},{8,10},{9,11},{10,... | collective-permute-start | bytes 884744 | tf_op jit(solution)/shard_map/ppermute | solution.py:148
  369.7 10.6 %collective-permute-start.11 = (bf16[48,3,1024]{2,0,1:T(8,128)(2,1)S(1)}, bf16[48,3,1024]{2,0,1:T(8,128)(2,1)S(1)}, u32[]{:S(2)}, u32[]{:S(2)}) collective-permute-start(bf16[48,3,1024]{2,0,1:T(8,128)(2,1)S(1)} %get-tuple-element.68), channel_id=1, source_target_pairs={{0,3},{1,0},{2,1},{3,2},{4,7},{5,4},{6,5},{7,6},{8,11},{9,8},{10,9... | collective-permute-start | bytes 884744 | tf_op jit(solution)/shard_map/ppermute | solution.py:148
  369.7 10.6 %collective-permute-start.9 = (bf16[48,3,1024]{2,0,1:T(8,128)(2,1)S(1)}, bf16[48,3,1024]{2,0,1:T(8,128)(2,1)S(1)}, u32[]{:S(2)}, u32[]{:S(2)}) collective-permute-start(bf16[48,3,1024]{2,0,1:T(8,128)(2,1)S(1)} %get-tuple-element.67), channel_id=1, source_target_pairs={{0,1},{1,2},{2,3},{3,0},{4,5},{5,6},{6,7},{7,4},{8,9},{9,10},{10,1... | collective-permute-start | bytes 884744 | tf_op jit(solution)/shard_map/ppermute | solution.py:148
  380.5 21.9 %collective-permute-start.12 = (bf16[48,3,1024]{2,0,1:T(8,128)(2,1)S(1)}, bf16[48,3,1024]{2,0,1:T(8,128)(2,1)S(1)}, u32[]{:S(2)}, u32[]{:S(2)}) collective-permute-start(bf16[48,3,1024]{2,0,1:T(8,128)(2,1)S(1)} %add_convert_fusion), channel_id=1, source_target_pairs={{0,0},{1,4},{2,8},{3,12},{4,1},{5,5},{6,9},{7,13},{8,2},{9,6},{10,... | collective-permute-start | bytes 884744 | tf_op jit(solution)/shard_map/ppermute | solution.py:159
  384.0 27.6 %collective-permute-start.13 = (bf16[48,3,1024]{2,0,1:T(8,128)(2,1)S(1)}, bf16[48,3,1024]{2,0,1:T(8,128)(2,1)S(1)}, u32[]{:S(2)}, u32[]{:S(2)}) collective-permute-start(bf16[48,3,1024]{2,0,1:T(8,128)(2,1)S(1)} %add_convert_fusion), channel_id=1, source_target_pairs={{0,4},{1,8},{2,12},{3,0},{4,5},{5,9},{6,13},{7,1},{8,6},{9,10},{10... | collective-permute-start | bytes 884744 | tf_op jit(solution)/shard_map/ppermute | solution.py:159
  387.4 24.2 %collective-permute-start.14 = (bf16[48,3,1024]{2,0,1:T(8,128)(2,1)S(1)}, bf16[48,3,1024]{2,0,1:T(8,128)(2,1)S(1)}, u32[]{:S(2)}, u32[]{:S(2)}) collective-permute-start(bf16[48,3,1024]{2,0,1:T(8,128)(2,1)S(1)} %add_convert_fusion), channel_id=1, source_target_pairs={{0,8},{1,12},{2,0},{3,4},{4,9},{5,13},{6,1},{7,5},{8,10},{9,14},{1... | collective-permute-start | bytes 884744 | tf_op jit(solution)/shard_map/ppermute | solution.py:159
  387.6 25.2 %collective-permute-start.15 = (bf16[48,3,1024]{2,0,1:T(8,128)(2,1)S(1)}, bf16[48,3,1024]{2,0,1:T(8,128)(2,1)S(1)}, u32[]{:S(2)}, u32[]{:S(2)}) collective-permute-start(bf16[48,3,1024]{2,0,1:T(8,128)(2,1)S(1)} %add_convert_fusion), channel_id=1, source_target_pairs={{0,12},{1,0},{2,4},{3,8},{4,13},{5,1},{6,5},{7,9},{8,14},{9,2},{10... | collective-permute-start | bytes 884744 | tf_op jit(solution)/shard_map/ppermute | solution.py:159
  (16 other events, 177.4 us)
Sparse Core Ops, SparseCore 0:
  11.5 50.0 all-gather.4
  63.1 87.2 all-gather.6
  152.0 87.8 all-gather.8
  247.7 87.9 all-gather.10
where the time goes:
time: 431 us; the launch traced here: 424 us
  waiting for transfers between devices  239 us (55%)
  matrix products  63.5 us (15%)
  local copies, waits for them, and re-layouts  45.9 us (11%)
  other arithmetic  36.9 us (9%)
  starting transfers between devices  24.5 us (6%)
  between operations  14.3 us (3%)
    ppermute x3, waiting for transfers between devices, forward(): return lax.ppermute(onward, 'groups', [(0, 1), (1, 0)])  123 us
    all_gather x3, waiting for transfers between devices, moved_weights(): gathered = lax.all_gather(mine, 'video', axis=0, tiled=True)  77.6 us
    ppermute x4, waiting for transfers between devices, per_device(): got = lax.ppermute(clip_rows, ('video', 'tensor'), pairs)  24.4 us
    dot_general x3, matrix products, per_device(): jnp.dot(own_half, gathered.reshape(n_video * half, width), preferred_elem...  17.3 us
    dot_general x3, matrix products, per_device(): jnp.dot(rolled, received.reshape((n_video - 1) * half, width), preferred_...  16.6 us
    convert_element_type x1, other arithmetic, per_device(): normed = normed.astype(jnp.bfloat16).reshape(patch_rows, frames.shape[2])  12.2 us
    unnamed x55, local copies, waits for them, and re-layouts  11.3 us
    dot_general x1, matrix products, per_device(): proj = jnp.dot(normed, full, preferred_element_type=jnp.float32)  11 us
  transfers between devices with their start and end apart: 20, of which 13 were waited for; matrix products, arithmetic and copies ran while one was open for 28% of the time, Pallas kernels for 0%

commit v1 on v0

--- a/solution.py
+++ b/solution.py
@@ -27,7 +27,16 @@
     if after is not None:
         mine, after = lax.optimization_barrier((mine, after))
     other = lax.dynamic_slice_in_dim(chunk, (1 - g) * half, half, axis=0)
-    gathered = lax.all_gather(mine, "video", axis=0, tiled=True)
+    ways = lax.axis_size("video")
+    up = [(d, (d + 1) % ways) for d in range(ways)]
+    down = [(d, (d - 1) % ways) for d in range(ways)]
+    earlier, later = ([mine], [mine])
+    for __2 in range(ways // 2):
+        earlier.append(lax.ppermute(earlier[-1], "video", up))
+    for __2 in range((ways - 1) // 2):
+        later.append(lax.ppermute(later[-1], "video", down))
+    line = jnp.concatenate([*earlier[::-1], *later[1:]], axis=0)
+    gathered = jnp.roll(line, (lax.axis_index("video") - ways // 2) * mine.shape[0], axis=0)
     onward = jnp.concatenate(
         [
             lax.dynamic_slice_in_dim(gathered, (v + 1 + i) % n_video * half, half, axis=0)

time: 431 us -> 448 us (1.039)
  waiting for transfers between devices: 239 us -> 192 us
  local copies, waits for them, and re-layouts: 45.9 us -> 67.5 us
  starting transfers between devices: 24.5 us -> 44 us
  other arithmetic: 36.9 us -> 52.6 us
  matrix products: 63.5 us -> 70.6 us
    ppermute x0 -> x9, waiting for transfers between devices: none -> 90.7 us  [the longest x6 90.7 us: moved_weights(): earlier.append(lax.ppermute(earlier[-1], 'video', up))]
    all_gather x3 -> x0, waiting for transfers between devices: 77.6 us -> none  [moved_weights(): gathered = lax.all_gather(mine, 'video', axis=0, tiled=True)]
    ppermute x3, waiting for transfers between devices: 123 us -> 50.6 us  [forward(): return lax.ppermute(onward, 'groups', [(0, 1), (1, 0)])]
    ppermute x0 -> x9, starting transfers between devices: none -> 22.8 us  [the longest x6 19.5 us: moved_weights(): earlier.append(lax.ppermute(earlier[-1], 'video', up))]
    dynamic_slice x0 -> x3, local copies, waits for them, and re-layouts: none -> 13.9 us  [moved_weights(): jnp.roll(line, (lax.axis_index('video') - ways // 2) * mine.shape[0], axi...]
    concatenate x0 -> x2, other arithmetic: none -> 10.1 us  [moved_weights(): jnp.roll(line, (lax.axis_index('video') - ways // 2) * mine.shape[0], axi...]
    ppermute x3, waiting for transfers between devices: 0.01 us -> 9.31 us  [per_device(): lax.ppermute(frame_video, 'video', [(a, (a + k) % n_video) for a in range...]
    dot_general x3, matrix products: 17.3 us -> 22.7 us  [per_device(): jnp.dot(own_half, gathered.reshape(n_video * half, width), preferred_elem...]
  transfers between devices with their start and end apart: 20 -> 26, of which waited for: 13 -> 18; matrix products, arithmetic and copies ran while one was open for 28% -> 33% of each run, Pallas kernels for 0% -> 0%
where the time goes in v1:
time: 448 us; the launch traced here: 442 us
  waiting for transfers between devices  192 us (43%)
  matrix products  70.6 us (16%)
  local copies, waits for them, and re-layouts  67.5 us (15%)
  other arithmetic  52.6 us (12%)
  starting transfers between devices  44 us (10%)
  between operations  14.5 us (3%)
    ppermute x6, waiting for transfers between devices, moved_weights(): earlier.append(lax.ppermute(earlier[-1], 'video', up))  90.7 us
    ppermute x3, waiting for transfers between devices, forward(): return lax.ppermute(onward, 'groups', [(0, 1), (1, 0)])  50.6 us
    ppermute x4, waiting for transfers between devices, per_device(): got = lax.ppermute(clip_rows, ('video', 'tensor'), pairs)  25.4 us
    dot_general x3, matrix products, per_device(): jnp.dot(own_half, gathered.reshape(n_video * half, width), preferred_elem...  22.7 us
    dot_general x3, matrix products, per_device(): jnp.dot(rolled, received.reshape((n_video - 1) * half, width), preferred_...  19.7 us
    ppermute x6, starting transfers between devices, moved_weights(): earlier.append(lax.ppermute(earlier[-1], 'video', up))  19.5 us
    unnamed x62, local copies, waits for them, and re-layouts  14 us
    dynamic_slice x3, local copies, waits for them, and re-layouts, moved_weights(): jnp.roll(line, (lax.axis_index('video') - ways // 2) * mine.shape[0], axi...  13.9 us
  transfers between devices with their start and end apart: 26, of which 18 were waited for; matrix products, arithmetic and copies ran while one was open for 33% of the time, Pallas kernels for 0%

profile of v1, /device:TPU:10, one launch (start us, length us, event | category | flops | bytes accessed | tf_op | source)
XLA Modules:
  0.0 441.6 jit_solution(2055930263515296257)
XLA Ops:
  12.6 14.3 %collective-permute-done = bf16[768,3,128]{0,2,1:T(8,128)(2,1)} collective-permute-done((bf16[768,3,128]{0,2,1:T(8,128)(2,1)S(1)}, bf16[768,3,128]{0,2,1:T(8,128)(2,1)}, u32[]{:S(2)}, u32[]{:S(2)}) %collective-permute-start) | collective-permute-done | bytes 589856 | tf_op jit(solution)/shard_map/ppermute | solution.py:35
  26.9 12.0 %collective-permute-start.1 = (bf16[768,3,128]{0,2,1:T(8,128)(2,1)}, bf16[768,3,128]{0,2,1:T(8,128)(2,1)}, u32[]{:S(2)}, u32[]{:S(2)}) collective-permute-start(bf16[768,3,128]{0,2,1:T(8,128)(2,1)} %collective-permute-done), channel_id=1, source_target_pairs={{0,4},{4,8},{8,12},{12,0},{1,5},{5,9},{9,13},{13,1},{2,6},{6,10},{... | collective-permute-start | bytes 1769480 | tf_op jit(solution)/shard_map/ppermute | solution.py:35
  43.0 8.1 %collective-permute-done.1 = bf16[768,3,128]{0,2,1:T(8,128)(2,1)} collective-permute-done((bf16[768,3,128]{0,2,1:T(8,128)(2,1)}, bf16[768,3,128]{0,2,1:T(8,128)(2,1)}, u32[]{:S(2)}, u32[]{:S(2)}) %collective-permute-start.1) | collective-permute-done | bytes 589856 | tf_op jit(solution)/shard_map/ppermute | solution.py:35
  73.6 5.0 %collective-permute-start.9 = (s32[3]{0:T(128)S(1)}, s32[3]{0:T(128)S(1)}, u32[]{:S(2)}, u32[]{:S(2)}) collective-permute-start(s32[3]{0:T(128)S(1)} %copy-done.15), channel_id=1, source_target_pairs={{0,8},{4,12},{8,0},{12,4},{1,9},{5,13},{9,1},{13,5},{2,10},{6,14},... | collective-permute-start | bytes 44 | tf_op jit(solution)/shard_map/ppermute | solution.py:113
  88.5 8.2 %collective-permute-done.8 = s32[3]{0:T(128)S(1)} collective-permute-done((s32[3]{0:T(128)S(1)}, s32[3]{0:T(128)S(1)}, u32[]{:S(2)}, u32[]{:S(2)}) %collective-permute-start.8) | collective-permute-done | bytes 44 | tf_op jit(solution)/shard_map/ppermute | solution.py:113
  100.7 5.0 %convert_reduce_fusion = f32[3,256]{1,0:T(4,128)S(1)} fusion(bf16[3,256,6144]{2,1,0:T(8,128)(2,1)} %param.6), kind=kLoop, calls=%fused_computation.4 | loop fusion | flops 9436416 | bytes 9440256 | tf_op jit(solution)/shard_map/reduce_sum | solution.py:96
  105.7 6.3 %fusion.2 = f32[3,256]{1,0:T(4,128)S(1)} fusion(bf16[3,256,6144]{2,1,0:T(8,128)(2,1)} %param.6, f32[3,256]{1,0:T(4,128)S(1)} %broadcast_multiply_fusion), kind=kLoop, calls=%fused_computation.7 | loop fusion | flops 18873600 | bytes 9443328 | tf_op jit(solution)/shard_map/reduce_sum | solution.py:97
  112.0 12.2 %fusion.3 = bf16[3,256,6144]{2,1,0:T(8,128)(2,1)} fusion(bf16[3,256,6144]{2,1,0:T(8,128)(2,1)} %param.6, f32[3,256]{1,0:T(4,128)S(1)} %add_rsqrt_fusion.10, f32[3,256]{1,0:T(4,128)S(1)} %broadcast_multiply_fusion), kind=kLoop, calls=%fused_computation.8 | loop fusion | flops 18874368 | bytes 18880512 | tf_op jit(solution)/shard_map/convert_element_type | solution.py:98
  129.4 20.2 %collective-permute-done.5 = bf16[768,3,256]{0,2,1:T(8,128)(2,1)} collective-permute-done((bf16[768,3,256]{0,2,1:T(8,128)(2,1)}, bf16[768,3,256]{0,2,1:T(8,128)(2,1)}, u32[]{:S(2)}, u32[]{:S(2)}) %collective-permute-start.5) | collective-permute-done | bytes 1179680 | tf_op jit(solution)/shard_map/ppermute | solution.py:35
  149.6 6.2 %maximum_maximum_fusion = bf16[6144,3,256]{0,2,1:T(8,128)(2,1)S(1)} fusion(bf16[768,3,256]{0,2,1:T(8,128)(2,1)} %copy-done.6, bf16[768,3,256]{0,2,1:T(8,128)(2,1)S(1)} %copy.173, bf16[768,3,256]{0,2,1:T(8,128)(2,1)} %collective-permute-done.4, bf16[768,3,256]{0,2,1:T(8,128)(2,1)} %collective-permute-done.5), kind=kLoop, calls=%fused_computation.9 | loop fusion | flops 75497472 | bytes 14155776 | tf_op jit(solution)/shard_map/jit(_roll_dynamic)/concatenate | solution.py:39
  167.5 5.5 %pad_maximum_fusion = bf16[768,3072]{1,0:T(8,128)(2,1)} fusion(bf16[768,768]{1,0:T(8,128)(2,1)} %get-tuple-element.41, bf16[768,768]{1,0:T(8,128)(2,1)} %get-tuple-element.42, bf16[768,768]{1,0:T(8,128)(2,1)} %get-tuple-element.43, bf16[768,768]{1,0:T(8,128)(2,1)} %get-tuple-element.44), kind=kLoop, calls=%fused_computation.13 | loop fusion | flops 18874368 | bytes 9437184 | tf_op jit(solution)/shard_map/concatenate | solution.py:105
  176.4 33.6 %collective-permute-done.11 = bf16[768,3,256]{0,2,1:T(8,128)(2,1)} collective-permute-done((bf16[768,3,256]{0,2,1:T(8,128)(2,1)S(1)}, bf16[768,3,256]{0,2,1:T(8,128)(2,1)}, u32[]{:S(2)}, u32[]{:S(2)}) %collective-permute-start.11) | collective-permute-done | bytes 1179680 | tf_op jit(solution)/shard_map/ppermute | solution.py:35
  222.2 14.5 %collective-permute-done.12 = bf16[768,3,256]{0,2,1:T(8,128)(2,1)S(1)} collective-permute-done((bf16[768,3,256]{0,2,1:T(8,128)(2,1)}, bf16[768,3,256]{0,2,1:T(8,128)(2,1)S(1)}, u32[]{:S(2)}, u32[]{:S(2)}) %collective-permute-start.12) | collective-permute-done | bytes 1179680 | tf_op jit(solution)/shard_map/ppermute | solution.py:35
  249.9 45.2 %collective-permute-done.7 = bf16[2304,3,256]{0,2,1:T(8,128)(2,1)} collective-permute-done((bf16[2304,3,256]{0,2,1:T(8,128)(2,1)}, bf16[2304,3,256]{0,2,1:T(8,128)(2,1)}, u32[]{:S(2)}, u32[]{:S(2)}) %collective-permute-start.7) | collective-permute-done | bytes 3538976 | tf_op jit(solution)/shard_map/ppermute | solution.py:51
  295.2 6.4 %fusion.12 = f32[768,384]{1,0:T(8,128)} fusion(f32[768,384]{1,0:T(8,128)} %fusion.65, f32[768,384]{1,0:T(8,128)S(1)} %copy-done.7, bf16[768,3072]{1,0:T(8,128)(2,1)} %pad_maximum_fusion, bf16[3072,384]{0,1:T(8,128)(2,1)S(1)} %bitcast.195), kind=kOutput, calls=%fused_computation.28 | convolution fusion | flops 1812529152 | bytes 10616832 | tf_op jit(solution)/shard_map/dot_general | solution.py:130
  307.1 9.0 %fusion.72 = f32[768,768]{1,0:T(8,128)} fusion(bf16[768,3072]{1,0:T(8,128)(2,1)} %pad_maximum_fusion, bf16[3072,768]{0,1:T(8,128)(2,1)} %bitcast.191), kind=kOutput, calls=%fused_computation.193 | convolution fusion | flops 3623878656 | bytes 11796480 | tf_op jit(solution)/shard_map/dot_general | solution.py:130
  317.8 8.8 %add_add_fusion.1 = f32[768,768]{1,0:T(8,128)} fusion(f32[768,768]{1,0:T(8,128)} %fusion.22, f32[768,768]{1,0:T(8,128)} %fusion.72, bf16[2304,768]{0,1:T(8,128)(2,1)} %bitcast.21, bf16[768,768]{1,0:T(8,128)(2,1)} %get-tuple-element.39, bf16[768,768]{1,0:T(8,128)(2,1)} %get-tuple-element.40, bf16[768,768]{1,0:T(8,128)(2,1)} %get-tuple-element.38), kind=kOutput, calls=%fused_computation.19 | convolution fusion | flops 2729705472 | bytes 14155776 | tf_op jit(solution)/shard_map/dot_general | solution.py:133
  333.8 7.3 %fusion.73 = f32[768,768]{1,0:T(8,128)S(1)} fusion(bf16[768,3072]{1,0:T(8,128)(2,1)} %pad_maximum_fusion, bf16[3072,768]{0,1:T(8,128)(2,1)} %bitcast.192), kind=kOutput, calls=%fused_computation.194 | convolution fusion | flops 3623878656 | bytes 11796480 | tf_op jit(solution)/shard_map/dot_general | solution.py:130
  341.0 5.3 %collective-permute-done.14 = bf16[2304,3,256]{0,2,1:T(8,128)(2,1)} collective-permute-done((bf16[2304,3,256]{0,2,1:T(8,128)(2,1)}, bf16[2304,3,256]{0,2,1:T(8,128)(2,1)}, u32[]{:S(2)}, u32[]{:S(2)}) %collective-permute-start.14) | collective-permute-done | bytes 3538976 | tf_op jit(solution)/shard_map/ppermute | solution.py:51
  346.4 6.4 %add_add_fusion = f32[768,768]{1,0:T(8,128)} fusion(f32[768,768]{1,0:T(8,128)S(1)} %copy-done.16, f32[768,768]{1,0:T(8,128)S(1)} %fusion.73, bf16[2304,768]{0,1:T(8,128)(2,1)} %bitcast.29, bf16[768,768]{1,0:T(8,128)(2,1)S(1)} %copy-done.12, bf16[768,768]{1,0:T(8,128)(2,1)S(1)} %copy-done.14, bf16[768,768]{1,0:T(8,128)(2,1)S(1)} %copy-done.10), kind=kOutput, calls=%fused_computation.18 | convolution fusion | flops 2729705472 | bytes 14155776 | tf_op jit(solution)/shard_map/dot_general | solution.py:133
  359.7 11.0 %fusion.7 = f32[3,256,3,1,128]{1,4,2,0,3:T(8,128)S(1)} fusion(bf16[6144,3,128]{0,2,1:T(8,128)(2,1)} %all-gather.2.cloned.1.call-done, bf16[3,256,6144]{2,1,0:T(8,128)(2,1)} %fusion.3), kind=kOutput, calls=%fused_computation.26 | convolution fusion | flops 3623878656 | bytes 15335424 | tf_op jit(solution)/shard_map/dot_general | solution.py:123
  385.3 6.7 %collective-permute-done.18 = bf16[48,3,1024]{2,0,1:T(8,128)(2,1)S(1)} collective-permute-done((bf16[48,3,1024]{2,0,1:T(8,128)(2,1)S(1)}, bf16[48,3,1024]{2,0,1:T(8,128)(2,1)S(1)}, u32[]{:S(2)}, u32[]{:S(2)}) %collective-permute-start.18) | collective-permute-done | bytes 294944 | tf_op jit(solution)/shard_map/ppermute | solution.py:157
  404.8 14.1 %collective-permute-done.21 = bf16[48,3,1024]{2,0,1:T(8,128)(2,1)S(1)} collective-permute-done((bf16[48,3,1024]{2,0,1:T(8,128)(2,1)S(1)}, bf16[48,3,1024]{2,0,1:T(8,128)(2,1)S(1)}, u32[]{:S(2)}, u32[]{:S(2)}) %collective-permute-start.21) | collective-permute-done | bytes 294944 | tf_op jit(solution)/shard_map/ppermute | solution.py:168
  418.9 9.3 %collective-permute-done.22 = bf16[48,3,1024]{2,0,1:T(8,128)(2,1)S(1)} collective-permute-done((bf16[48,3,1024]{2,0,1:T(8,128)(2,1)S(1)}, bf16[48,3,1024]{2,0,1:T(8,128)(2,1)S(1)}, u32[]{:S(2)}, u32[]{:S(2)}) %collective-permute-start.22) | collective-permute-done | bytes 294944 | tf_op jit(solution)/shard_map/ppermute | solution.py:168
  (215 shorter events, 146.5 us)
Async XLA Ops:
  6.5 353.2 %all-gather.2.cloned.1.call-start = ((), (), s32[]{:S(2)}) async-start(), calls=%async_computation | async-start | bytes 5898240 | tf_op jit(solution)/shard_map/all_gather | solution.py:86
  10.5 16.4 %collective-permute-start = (bf16[768,3,128]{0,2,1:T(8,128)(2,1)S(1)}, bf16[768,3,128]{0,2,1:T(8,128)(2,1)}, u32[]{:S(2)}, u32[]{:S(2)}) collective-permute-start(bf16[768,3,128]{0,2,1:T(8,128)(2,1)S(1)} %copy.170), channel_id=1, source_target_pairs={{0,4},{4,8},{8,12},{12,0},{1,5},{5,9},{9,13},{13,1},{2,6},{6,10},{... | collective-permute-start | bytes 1769480 | tf_op jit(solution)/shard_map/ppermute | solution.py:35
  12.1 41.3 %collective-permute-start.2 = (bf16[768,3,128]{0,2,1:T(8,128)(2,1)S(1)}, bf16[768,3,128]{0,2,1:T(8,128)(2,1)S(1)}, u32[]{:S(2)}, u32[]{:S(2)}) collective-permute-start(bf16[768,3,128]{0,2,1:T(8,128)(2,1)S(1)} %copy.170), channel_id=1, source_target_pairs={{0,12},{4,0},{8,4},{12,8},{1,13},{5,1},{9,5},{13,9},{2,14},{6,2},{... | collective-permute-start | bytes 1769480 | tf_op jit(solution)/shard_map/ppermute | solution.py:37
  26.9 24.2 %collective-permute-start.1 = (bf16[768,3,128]{0,2,1:T(8,128)(2,1)}, bf16[768,3,128]{0,2,1:T(8,128)(2,1)}, u32[]{:S(2)}, u32[]{:S(2)}) collective-permute-start(bf16[768,3,128]{0,2,1:T(8,128)(2,1)} %collective-permute-done), channel_id=1, source_target_pairs={{0,4},{4,8},{8,12},{12,0},{1,5},{5,9},{9,13},{13,1},{2,6},{6,10},{... | collective-permute-start | bytes 1769480 | tf_op jit(solution)/shard_map/ppermute | solution.py:35
  60.4 40.2 %collective-permute-start.3 = (bf16[2304,3,128]{0,2,1:T(8,128)(2,1)}, bf16[2304,3,128]{0,2,1:T(8,128)(2,1)}, u32[]{:S(2)}, u32[]{:S(2)}) collective-permute-start(bf16[2304,3,128]{0,2,1:T(8,128)(2,1)} %pad_maximum_fusion.4), channel_id=1, source_target_pairs={{0,16},{16,0},{1,17},{17,1},{2,18},{18,2},{3,19},{19,3},{4,20},{20... | collective-permute-start | bytes 5308424 | tf_op jit(solution)/shard_map/ppermute | solution.py:51
  70.0 30.1 %collective-permute-start.4 = (bf16[768,3,256]{0,2,1:T(8,128)(2,1)S(1)}, bf16[768,3,256]{0,2,1:T(8,128)(2,1)}, u32[]{:S(2)}, u32[]{:S(2)}) collective-permute-start(bf16[768,3,256]{0,2,1:T(8,128)(2,1)S(1)} %copy.173), channel_id=1, source_target_pairs={{0,4},{4,8},{8,12},{12,0},{1,5},{5,9},{9,13},{13,1},{2,6},{6,10},{... | collective-permute-start | bytes 3538952 | tf_op jit(solution)/shard_map/ppermute | solution.py:35
  71.5 16.9 %collective-permute-start.10 = (s32[3]{0:T(128)S(1)}, s32[3]{0:T(128)S(1)}, u32[]{:S(2)}, u32[]{:S(2)}) collective-permute-start(s32[3]{0:T(128)S(1)} %copy-done.15), channel_id=1, source_target_pairs={{0,12},{4,0},{8,4},{12,8},{1,13},{5,1},{9,5},{13,9},{2,14},{6,2},{... | collective-permute-start | bytes 44 | tf_op jit(solution)/shard_map/ppermute | solution.py:113
  72.3 24.4 %collective-permute-start.8 = (s32[3]{0:T(128)S(1)}, s32[3]{0:T(128)S(1)}, u32[]{:S(2)}, u32[]{:S(2)}) collective-permute-start(s32[3]{0:T(128)S(1)} %copy-done.15), channel_id=1, source_target_pairs={{0,4},{4,8},{8,12},{12,0},{1,5},{5,9},{9,13},{13,1},{2,6},{6,10},{... | collective-permute-start | bytes 44 | tf_op jit(solution)/shard_map/ppermute | solution.py:113
  73.6 24.2 %collective-permute-start.9 = (s32[3]{0:T(128)S(1)}, s32[3]{0:T(128)S(1)}, u32[]{:S(2)}, u32[]{:S(2)}) collective-permute-start(s32[3]{0:T(128)S(1)} %copy-done.15), channel_id=1, source_target_pairs={{0,8},{4,12},{8,0},{12,4},{1,9},{5,13},{9,1},{13,5},{2,10},{6,14},... | collective-permute-start | bytes 44 | tf_op jit(solution)/shard_map/ppermute | solution.py:113
  98.5 29.8 %collective-permute-start.6 = (bf16[768,3,256]{0,2,1:T(8,128)(2,1)S(1)}, bf16[768,3,256]{0,2,1:T(8,128)(2,1)S(1)}, u32[]{:S(2)}, u32[]{:S(2)}) collective-permute-start(bf16[768,3,256]{0,2,1:T(8,128)(2,1)S(1)} %copy.173), channel_id=1, source_target_pairs={{0,12},{4,0},{8,4},{12,8},{1,13},{5,1},{9,5},{13,9},{2,14},{6,2},{... | collective-permute-start | bytes 3538952 | tf_op jit(solution)/shard_map/ppermute | solution.py:37
  100.1 49.5 %collective-permute-start.5 = (bf16[768,3,256]{0,2,1:T(8,128)(2,1)}, bf16[768,3,256]{0,2,1:T(8,128)(2,1)}, u32[]{:S(2)}, u32[]{:S(2)}) collective-permute-start(bf16[768,3,256]{0,2,1:T(8,128)(2,1)} %collective-permute-done.4), channel_id=1, source_target_pairs={{0,4},{4,8},{8,12},{12,0},{1,5},{5,9},{9,13},{13,1},{2,6},{6,10},{... | collective-permute-start | bytes 3538952 | tf_op jit(solution)/shard_map/ppermute | solution.py:35
  160.7 49.3 %collective-permute-start.11 = (bf16[768,3,256]{0,2,1:T(8,128)(2,1)S(1)}, bf16[768,3,256]{0,2,1:T(8,128)(2,1)}, u32[]{:S(2)}, u32[]{:S(2)}) collective-permute-start(bf16[768,3,256]{0,2,1:T(8,128)(2,1)S(1)} %copy-done.1), channel_id=1, source_target_pairs={{0,4},{4,8},{8,12},{12,0},{1,5},{5,9},{9,13},{13,1},{2,6},{6,10},{... | collective-permute-start | bytes 3538952 | tf_op jit(solution)/shard_map/ppermute | solution.py:35
  173.0 49.2 %collective-permute-start.13 = (bf16[768,3,256]{0,2,1:T(8,128)(2,1)S(1)}, bf16[768,3,256]{0,2,1:T(8,128)(2,1)S(1)}, u32[]{:S(2)}, u32[]{:S(2)}) collective-permute-start(bf16[768,3,256]{0,2,1:T(8,128)(2,1)S(1)} %copy-done.1), channel_id=1, source_target_pairs={{0,12},{4,0},{8,4},{12,8},{1,13},{5,1},{9,5},{13,9},{2,14},{6,2},{... | collective-permute-start | bytes 3538952 | tf_op jit(solution)/shard_map/ppermute | solution.py:37
  210.0 26.7 %collective-permute-start.12 = (bf16[768,3,256]{0,2,1:T(8,128)(2,1)}, bf16[768,3,256]{0,2,1:T(8,128)(2,1)S(1)}, u32[]{:S(2)}, u32[]{:S(2)}) collective-permute-start(bf16[768,3,256]{0,2,1:T(8,128)(2,1)} %collective-permute-done.11), channel_id=1, source_target_pairs={{0,4},{4,8},{8,12},{12,0},{1,5},{5,9},{9,13},{13,1},{2,6},{6,10},{... | collective-permute-start | bytes 3538952 | tf_op jit(solution)/shard_map/ppermute | solution.py:35
  215.4 79.8 %collective-permute-start.7 = (bf16[2304,3,256]{0,2,1:T(8,128)(2,1)}, bf16[2304,3,256]{0,2,1:T(8,128)(2,1)}, u32[]{:S(2)}, u32[]{:S(2)}) collective-permute-start(bf16[2304,3,256]{0,2,1:T(8,128)(2,1)} %pad_maximum_fusion.1), channel_id=1, source_target_pairs={{0,16},{16,0},{1,17},{17,1},{2,18},{18,2},{3,19},{19,3},{4,20},{20... | collective-permute-start | bytes 10616840 | tf_op jit(solution)/shard_map/ppermute | solution.py:51
  244.5 101.9 %collective-permute-start.14 = (bf16[2304,3,256]{0,2,1:T(8,128)(2,1)}, bf16[2304,3,256]{0,2,1:T(8,128)(2,1)}, u32[]{:S(2)}, u32[]{:S(2)}) collective-permute-start(bf16[2304,3,256]{0,2,1:T(8,128)(2,1)} %pad_maximum_fusion.3), channel_id=1, source_target_pairs={{0,16},{16,0},{1,17},{17,1},{2,18},{18,2},{3,19},{19,3},{4,20},{20... | collective-permute-start | bytes 10616840 | tf_op jit(solution)/shard_map/ppermute | solution.py:51
  373.1 5.8 %collective-permute-start.17 = (bf16[48,768]{1,0:T(8,128)(2,1)S(1)}, bf16[48,768]{1,0:T(8,128)(2,1)S(1)}, u32[]{:S(2)}, u32[]{:S(2)}) collective-permute-start(bf16[48,768]{1,0:T(8,128)(2,1)S(1)} %get-tuple-element.74), channel_id=1, source_target_pairs={{0,12},{4,0},{8,4},{12,8},{1,13},{5,1},{9,5},{13,9},{2,14},{6,2},{... | collective-permute-start | bytes 221192 | tf_op jit(solution)/shard_map/ppermute | solution.py:141
  383.2 8.8 %collective-permute-start.18 = (bf16[48,3,1024]{2,0,1:T(8,128)(2,1)S(1)}, bf16[48,3,1024]{2,0,1:T(8,128)(2,1)S(1)}, u32[]{:S(2)}, u32[]{:S(2)}) collective-permute-start(bf16[48,3,1024]{2,0,1:T(8,128)(2,1)S(1)} %get-tuple-element.68), channel_id=1, source_target_pairs={{0,1},{1,2},{2,3},{3,0},{4,5},{5,6},{6,7},{7,4},{8,9},{9,10},{10,1... | collective-permute-start | bytes 884744 | tf_op jit(solution)/shard_map/ppermute | solution.py:157
  383.3 9.9 %collective-permute-start.19 = (bf16[48,3,1024]{2,0,1:T(8,128)(2,1)S(1)}, bf16[48,3,1024]{2,0,1:T(8,128)(2,1)S(1)}, u32[]{:S(2)}, u32[]{:S(2)}) collective-permute-start(bf16[48,3,1024]{2,0,1:T(8,128)(2,1)S(1)} %get-tuple-element.70), channel_id=1, source_target_pairs={{0,2},{1,3},{2,0},{3,1},{4,6},{5,7},{6,4},{7,5},{8,10},{9,11},{10,... | collective-permute-start | bytes 884744 | tf_op jit(solution)/shard_map/ppermute | solution.py:157
  383.9 13.1 %collective-permute-start.20 = (bf16[48,3,1024]{2,0,1:T(8,128)(2,1)S(1)}, bf16[48,3,1024]{2,0,1:T(8,128)(2,1)S(1)}, u32[]{:S(2)}, u32[]{:S(2)}) collective-permute-start(bf16[48,3,1024]{2,0,1:T(8,128)(2,1)S(1)} %get-tuple-element.69), channel_id=1, source_target_pairs={{0,3},{1,0},{2,1},{3,2},{4,7},{5,4},{6,5},{7,6},{8,11},{9,8},{10,9... | collective-permute-start | bytes 884744 | tf_op jit(solution)/shard_map/ppermute | solution.py:157
  397.2 21.8 %collective-permute-start.21 = (bf16[48,3,1024]{2,0,1:T(8,128)(2,1)S(1)}, bf16[48,3,1024]{2,0,1:T(8,128)(2,1)S(1)}, u32[]{:S(2)}, u32[]{:S(2)}) collective-permute-start(bf16[48,3,1024]{2,0,1:T(8,128)(2,1)S(1)} %add_convert_fusion), channel_id=1, source_target_pairs={{0,0},{1,4},{2,8},{3,12},{4,1},{5,5},{6,9},{7,13},{8,2},{9,6},{10,... | collective-permute-start | bytes 884744 | tf_op jit(solution)/shard_map/ppermute | solution.py:168
  401.4 26.9 %collective-permute-start.22 = (bf16[48,3,1024]{2,0,1:T(8,128)(2,1)S(1)}, bf16[48,3,1024]{2,0,1:T(8,128)(2,1)S(1)}, u32[]{:S(2)}, u32[]{:S(2)}) collective-permute-start(bf16[48,3,1024]{2,0,1:T(8,128)(2,1)S(1)} %add_convert_fusion), channel_id=1, source_target_pairs={{0,4},{1,8},{2,12},{3,0},{4,5},{5,9},{6,13},{7,1},{8,6},{9,10},{10... | collective-permute-start | bytes 884744 | tf_op jit(solution)/shard_map/ppermute | solution.py:168
  404.1 24.2 %collective-permute-start.23 = (bf16[48,3,1024]{2,0,1:T(8,128)(2,1)S(1)}, bf16[48,3,1024]{2,0,1:T(8,128)(2,1)S(1)}, u32[]{:S(2)}, u32[]{:S(2)}) collective-permute-start(bf16[48,3,1024]{2,0,1:T(8,128)(2,1)S(1)} %add_convert_fusion), channel_id=1, source_target_pairs={{0,8},{1,12},{2,0},{3,4},{4,9},{5,13},{6,1},{7,5},{8,10},{9,14},{1... | collective-permute-start | bytes 884744 | tf_op jit(solution)/shard_map/ppermute | solution.py:168
  404.1 26.2 %collective-permute-start.24 = (bf16[48,3,1024]{2,0,1:T(8,128)(2,1)S(1)}, bf16[48,3,1024]{2,0,1:T(8,128)(2,1)S(1)}, u32[]{:S(2)}, u32[]{:S(2)}) collective-permute-start(bf16[48,3,1024]{2,0,1:T(8,128)(2,1)S(1)} %add_convert_fusion), channel_id=1, source_target_pairs={{0,12},{1,0},{2,4},{3,8},{4,13},{5,1},{6,5},{7,9},{8,14},{9,2},{10... | collective-permute-start | bytes 884744 | tf_op jit(solution)/shard_map/ppermute | solution.py:168
  (22 other events, 251.3 us)
Sparse Core Ops, SparseCore 0:
  250.0 87.8 all-gather.1
